TPU v7x, 128 devices: a whole 4x4x4 slice. The times are simulated.
128 devices in a mesh: wide: 64 (over z, y, x), narrow: 2 (over core).
Axes of the slice: x: 4, y: 4, z: 4, core: 2. Of those that a mesh axis runs over, the one named last changes fastest.
Arguments:
- tokens: bfloat16 [65536, 2048], P('wide', 'narrow'), may hold values from -6 to 6
- attn_gain: bfloat16 [2048], replicated, may hold values from 0.5 to 1.5
- q_weight: bfloat16 [2048, 3072], P('wide', 'narrow'), may hold values from -6 to 6
- kva_weight: bfloat16 [2048, 576], P('wide'), may hold values from -0.125 to 0.125
- kv_gain: bfloat16 [512], replicated, may hold values from 0.5 to 1.5
- kvb_weight: bfloat16 [512, 4096], P(None, 'narrow'), may hold values from -0.25 to 0.25
- o_weight: bfloat16 [2048, 2048], P('narrow'), may hold values from -0.125 to 0.125
- adapter_down: bfloat16 [2048, 1024], P(None, 'narrow'), may hold values from -0.125 to 0.125
- adapter_up_weight: bfloat16 [1024, 3072], P(None, 'narrow'), may hold values from -1.5 to 1.5
- lengths: int32 [64, 4], P('wide'), may hold values from 1 to 512, 1024 in all within a row
- adapter_ids: int32 [64, 4], P('wide'), may hold values from 0 to 63
- adapter_slot: int32 [64], replicated, may hold values from 0 to 63, each once
Outputs:
- hidden: bfloat16 [65536, 2048], P('wide', 'narrow')
- latent_cache: bfloat16 [65536, 576], P('wide')
Inputs may be any that keep to these rules, and one draw needn't show every extreme that they name: Each row of lengths sums to 1024, and its longest prompt is exactly 512.
All inputs are finite; a program needn't handle non-finite values.
Results may differ from a plain program's by a relative error of at most 0.0095.
The roundings to bfloat16 on the way count: a program that leaves them out, or rounds other values in their place, can miss the bound.
Values may be sent and summed in bfloat16 or wider, within the bound.
No kernel may reach another device: no remote copies, remote signals or barrier semaphores. Data moves between devices by JAX's collectives and lax.ppermute only.
A program may use at most 192 MiB of HBM per device.

v0:
```python
import jax
import jax.numpy as jnp
from jax import lax
from jax.sharding import PartitionSpec as P

NOPE = 128
ROPE = 64
VDIM = 128
LATENT = 512
RANK = 16
EPS = 1e-06
THETA = 50000.0
ADAPTER_SCALE = 2.0


def rms_scale(values, gain):
    mean_sq = jnp.mean(values * values, axis=-1, keepdims=True)
    return values * lax.rsqrt(mean_sq + EPS) * gain.astype(jnp.float32)


def rotate(values, positions):
    half = values.shape[-1] // 2
    freqs = jnp.exp(-jnp.log(THETA) * 2.0 * jnp.arange(half).astype(jnp.float32) / (2 * half))
    angle = positions.astype(jnp.float32)[:, None] * freqs[None, :]
    cosine = jnp.cos(angle)
    sine = jnp.sin(angle)
    if values.ndim == 3:
        cosine = cosine[:, None, :]
        sine = sine[:, None, :]
    first = values[..., :half]
    second = values[..., half:]
    return jnp.concatenate(
        [first * cosine - second * sine, first * sine + second * cosine], axis=-1
    )


def token_tables(length_row, id_row, adapter_slot, local_pos):
    ends = jnp.cumsum(length_row)
    starts = ends - length_row
    prompt = jnp.sum((ends[None, :] <= local_pos[:, None]).astype(jnp.int32), axis=1)
    onehot = (prompt[:, None] == jnp.arange(length_row.shape[0])[None, :]).astype(jnp.int32)
    position = local_pos - jnp.sum(onehot * starts[None, :], axis=1)
    adapter = jnp.sum(onehot * id_row[None, :], axis=1)
    slot_hot = (adapter[:, None] == jnp.arange(adapter_slot.shape[0])[None, :]).astype(jnp.int32)
    slot = jnp.sum(slot_hot * adapter_slot[None, :], axis=1)
    return (prompt, position, adapter, slot)


def swap(values):
    return lax.ppermute(values, "narrow", perm=[(0, 1), (1, 0)])


def body(
    tokens,
    attn_gain,
    q_weight,
    kva_weight,
    kv_gain,
    kvb_weight,
    o_weight,
    adapter_down,
    adapter_up_weight,
    lengths,
    adapter_ids,
    adapter_slot,
):
    rows = tokens.shape[0]
    half_width = tokens.shape[1]
    heads_here = o_weight.shape[0] // VDIM
    prompts_here = lengths.shape[1]
    q_cols = q_weight.shape[1]
    me = lax.axis_index("narrow")
    mine_first = me == 0
    joined = jnp.concatenate([q_weight, kva_weight], axis=1)
    joined = lax.all_gather(joined, "wide", axis=0, tiled=True)
    other = swap(tokens)
    whole = jnp.concatenate(
        [jnp.where(mine_first, tokens, other), jnp.where(mine_first, other, tokens)], axis=1
    )
    slots_here = adapter_down.shape[1] // RANK
    prompt_ids = adapter_ids[0]
    id_hot = (prompt_ids[:, None] == jnp.arange(adapter_slot.shape[0])[None, :]).astype(jnp.int32)
    prompt_slot = jnp.sum(id_hot * adapter_slot[None, :], axis=1)
    owner = prompt_slot // slots_here
    local_slot = prompt_slot % slots_here
    picked = jnp.concatenate(
        [
            lax.dynamic_slice_in_dim(adapter_down, local_slot[p] * RANK, RANK, 1)
            for p in range(prompts_here)
        ],
        axis=1,
    )
    picked_other = swap(picked)
    own_block = jnp.repeat(owner == me, RANK)
    chosen = jnp.where(own_block[None, :], picked, picked_other)
    normed = rms_scale(whole.astype(jnp.float32), attn_gain).astype(jnp.bfloat16)
    local_pos = jnp.arange(rows)
    prompt, position, adapter, slot = token_tables(
        lengths[0], adapter_ids[0], adapter_slot, local_pos
    )
    projections = jnp.dot(normed, joined, preferred_element_type=jnp.float32)
    query_vectors = projections[:, :q_cols]
    kv_pre = projections[:, q_cols:]
    member = (prompt[:, None] == jnp.arange(prompts_here)[None, :]).astype(jnp.float32)
    low = jnp.dot(normed, chosen, preferred_element_type=jnp.float32).reshape(
        rows, prompts_here, RANK
    )
    lowrank = jnp.sum(low * member[:, :, None], axis=1).astype(jnp.bfloat16)
    up_blocks = [
        lax.dynamic_slice_in_dim(adapter_up_weight, prompt_ids[prompt_index] * RANK, RANK, 0)
        for prompt_index in range(prompts_here)
    ]
    up_weight_rows = jnp.concatenate(up_blocks, axis=0)
    spread_rows = (member.astype(jnp.bfloat16)[:, :, None] * lowrank[:, None, :]).reshape(
        rows, prompts_here * RANK
    )
    query_vectors = query_vectors + ADAPTER_SCALE * jnp.dot(
        spread_rows, up_weight_rows, preferred_element_type=jnp.float32
    )
    query_vectors = query_vectors.reshape(rows, heads_here, NOPE + ROPE)
    query_vectors = jnp.concatenate(
        [query_vectors[..., :NOPE], rotate(query_vectors[..., NOPE:], position)], axis=-1
    ).astype(jnp.bfloat16)
    latent = rms_scale(kv_pre[:, :LATENT], kv_gain).astype(jnp.bfloat16)
    key_rope = rotate(kv_pre[:, LATENT:], position).astype(jnp.bfloat16)
    latent_cache = jnp.concatenate([latent, key_rope], axis=1)
    expanded = jnp.dot(latent, kvb_weight, preferred_element_type=jnp.float32).astype(jnp.bfloat16)
    expanded = expanded.reshape(rows, heads_here, NOPE + VDIM)
    key_nope = expanded[..., :NOPE]
    values = expanded[..., NOPE:]
    scale = 1.0 / jnp.sqrt(jnp.float32(NOPE + ROPE))
    scores = jnp.einsum(
        "qhd,khd->hqk", query_vectors[..., :NOPE], key_nope, preferred_element_type=jnp.float32
    )
    scores = scores + jnp.einsum(
        "qhd,kd->hqk", query_vectors[..., NOPE:], key_rope, preferred_element_type=jnp.float32
    )
    scores = scores * scale
    allowed = (prompt[None, :] == prompt[:, None]) & (local_pos[None, :] <= local_pos[:, None])
    scores = jnp.where(allowed[None, :, :], scores, jnp.float32(-1e30))
    top = jnp.max(scores, axis=-1, keepdims=True)
    expo = jnp.exp(scores - top)
    weights = (expo / jnp.sum(expo, axis=-1, keepdims=True)).astype(jnp.bfloat16)
    attended = jnp.einsum(
        "hqk,khd->qhd", weights, values, preferred_element_type=jnp.float32
    ).astype(jnp.bfloat16)
    attended = attended.reshape(rows, heads_here * VDIM)
    their_cols = lax.dynamic_slice_in_dim(o_weight, (1 - me) * half_width, half_width, 1)
    my_cols = lax.dynamic_slice_in_dim(o_weight, me * half_width, half_width, 1)
    theirs = jnp.dot(attended, their_cols, preferred_element_type=jnp.float32).astype(jnp.bfloat16)
    received = swap(theirs)
    mine = jnp.dot(attended, my_cols, preferred_element_type=jnp.float32).astype(jnp.bfloat16)
    projected = mine.astype(jnp.float32) + received.astype(jnp.float32)
    hidden = (tokens.astype(jnp.float32) + projected).astype(jnp.bfloat16)
    return (hidden, latent_cache)


def solution(mesh):
    return jax.shard_map(
        body,
        mesh=mesh,
        in_specs=(
            P("wide", "narrow"),
            P(),
            P("wide", "narrow"),
            P("wide", None),
            P(),
            P(None, "narrow"),
            P("narrow", None),
            P(None, "narrow"),
            P(None, "narrow"),
            P("wide", None),
            P("wide", None),
            P(),
        ),
        out_specs=(P("wide", "narrow"), P("wide", None)),
        check_vma=False,
    )
```

profile of v0, /device:TPU:1, one launch (start us, length us, event | category | flops | bytes accessed | tf_op | source)
XLA Modules:
  0.0 205.4 jit_solution(6438729907557349726)
XLA Ops:
  7.3 1.7 pad_maximum_fusion.3
  9.0 1.5 collective-permute-start
  14.4 2.5 %constant_dynamic-slice_fusion.7 = (bf16[2048,16]{1,0:T(8,128)(2,1)S(1)}, bf16[2048,16]{1,0:T(8,128)(2,1)S(1)}, bf16[2048,16]{1,0:T(8,128)(2,1)S(1)}, bf16[2048,16]{1,0:T(8,128)(2,1)S(1)}) fusion(bf16[2048,512]{1,0:T(8,128)(2,1)} %param.19, s32[]{:T(128)S(6)} %select_n.67, s32[]{:T(128)S(6)} %select_n.68, s32[]{:T(128)S(6)} %select_n.70, s32[]{:T(128)S(6)} %select_n.69), kind=kLoop, calls=%fused_computation.76 | loop fusion | bytes 524304 | tf_op jit(solution)/shard_map/dynamic_slice | solution.py:88
  16.9 1.5 pad_maximum_fusion.2
  23.2 1.5 constant_dynamic-slice_fusion.3
  25.3 2.5 %broadcast_select_fusion.1 = (bf16[1024,1024]{1,0:T(8,128)(2,1)S(1)}, bf16[1024,1024]{1,0:T(8,128)(2,1)S(1)}) fusion(bf16[1024,1024]{1,0:T(8,128)(2,1)} %param.12, bf16[1024,1024]{1,0:T(8,128)(2,1)} %collective-permute-done, pred[]{:T(512)S(6)} %eq.70), kind=kLoop, calls=%fused_computation.28 | loop fusion | flops 2097152 | bytes 8388609 | tf_op jit(solution)/shard_map/jit(_where)/select_n | solution.py:78
  28.8 3.1 %fusion.26 = f32[1024,64]{0,1:T(8,128)S(1)} fusion(bf16[2048,64]{1,0:T(8,128)(2,1)} %pad_maximum_fusion.2, bf16[2048,64]{1,0:T(8,128)(2,1)} %collective-permute-done.1, pred[64]{0:T(512)(128)(4,1)S(1)} %broadcast_in_dim.22, f32[2048]{0:T(1024)S(1)} %convert_element_type.94, f32[1024]{0:T(1024)S(1)} %add_rsqrt_fusion.1, ...), kind=kOutput, calls=%fused_computation.39 | convolution fusion | flops 283246592 | bytes 4993088 | tf_op jit(solution)/shard_map/dot_general | solution.py:105
  32.1 62.5 %all-gather.2.cloned.1.call-done = bf16[2048,2112]{1,0:T(8,128)(2,1)} async-done(((bf16[32,2112]{1,0:T(8,128)(2,1)}), bf16[2048,2112]{1,0:T(8,128)(2,1)}) %all-gather.2.cloned.1.call-update) | async-done | bytes 8650768 | tf_op jit(solution)/shard_map/all_gather | solution.py:75
  94.6 16.1 %fusion.47 = f32[1024,2112]{0,1:T(8,128)} fusion(bf16[2048,2112]{1,0:T(8,128)(2,1)} %all-gather.2.cloned.1.call-done, f32[2048]{0:T(1024)S(1)} %convert_element_type.94, f32[1024]{0:T(1024)S(1)} %add_rsqrt_fusion.1, bf16[1024,1024]{1,0:T(8,128)(2,1)} %copy-done.4, bf16[1024,1024]{1,0:T(8,128)(2,1)} %copy-done.3), kind=kOutput, calls=%fused_computation.91 | convolution fusion | flops 8873050112 | bytes 21508096 | tf_op jit(solution)/shard_map/dot_general | solution.py:101
  110.7 1.8 multiply_reduce_fusion
  112.4 1.8 multiply_convert_fusion
  114.3 2.4 %convolution_convert_fusion = bf16[1024,2048]{1,0:T(8,128)(2,1)S(1)} fusion(bf16[1024,512]{0,1:T(8,128)(2,1)S(1)} %multiply_convert_fusion, bf16[512,2048]{1,0:T(8,128)(2,1)S(1)} %copy-done), kind=kOutput, calls=%fused_computation.18 | convolution fusion | flops 2149580800 | bytes 7340032 | tf_op jit(solution)/shard_map/dot_general | solution.py:127
  116.7 1.5 copy.40
  118.3 1.6 fusion.49
  119.9 1.5 slice-done.2
  121.9 1.0 slice_add_fusion
  123.0 2.7 %copy-done.2 = f32[1024,1536]{0,1:T(8,128)} copy-done((f32[1024,1536]{0,1:T(8,128)}, f32[1024,1536]{0,1:T(8,128)S(1)}, u32[]{:S(2)}) %copy-start.2) | copy-done | bytes 6291480
  126.0 13.2 %fusion.22 = f32[1024,1024,8]{1,0,2:T(8,128)} fusion(bf16[1024,8,32]{0,2,1:T(8,128)(2,1)S(1)} %get-tuple-element.5, bf16[1024,8,32]{0,2,1:T(8,128)(2,1)S(1)} %get-tuple-element.4, bf16[1024,32]{0,1:T(8,128)(2,1)S(1)} %get-tuple-element.3, bf16[1024,32]{0,1:T(8,128)(2,1)S(1)} %get-tuple-element.2), kind=kOutput, calls=%fused_computation.32 | convolution fusion | flops 1076101120 | bytes 34734080 | tf_op jit(solution)/shard_map/qhd,kd->hqk/dot_general | solution.py:135
  139.2 26.8 %fusion.52 = (f32[8,1024]{1,0:T(8,128)S(1)}, f32[8,1024,1024]{1,2,0:T(8,128)}) fusion(f32[1024,1024,8]{1,0,2:T(8,128)} %fusion.22, pred[1024,1024]{0,1:T(8,128)(4,1)S(1)} %fusion.7, f32[1024,8,192]{0,2,1:T(8,128)} %bitcast.43, bf16[1024,8,128]{2,1,0:T(8,128)(2,1)S(1)} %get-tuple-element.7), kind=kOutput, calls=%fused_computation.95 | convolution fusion | flops 2189427712 | bytes 72384512 | tf_op jit(solution)/shard_map/sub | solution.py:142
  166.0 14.1 %fusion.17 = bf16[8,128,1024]{2,1,0:T(8,128)(2,1)} fusion(f32[8,1024,1024]{1,2,0:T(8,128)} %get-tuple-element.31, f32[8,1024]{1,0:T(8,128)S(1)} %get-tuple-element.30, bf16[1024,8,128]{2,1,0:T(8,128)(2,1)} %get-tuple-element.6), kind=kOutput, calls=%fused_computation.30 | convolution fusion | flops 2165309440 | bytes 37781504 | tf_op jit(solution)/shard_map/hqk,khd->qhd/dot_general | solution.py:144
  180.1 6.0 %fusion.14 = bf16[1024,1024]{1,0:T(8,128)(2,1)} fusion(bf16[1024,1024]{0,1:T(8,128)(2,1)} %bitcast.53, bf16[1024,2048]{1,0:T(8,128)(2,1)} %param.18, s32[]{:T(128)S(6)} %select_n.78), kind=kOutput, calls=%fused_computation.29 | convolution fusion | flops 2148532224 | bytes 6291460 | tf_op jit(solution)/shard_map/dot_general | solution.py:150
  186.8 1.1 pad_maximum_fusion.1
  187.9 3.0 %collective-permute-done.2 = bf16[1024,1024]{1,0:T(8,128)(2,1)} collective-permute-done((bf16[1024,1024]{1,0:T(8,128)(2,1)}, bf16[1024,1024]{1,0:T(8,128)(2,1)}, u32[]{:S(2)}, u32[]{:S(2)}) %collective-permute-start.2) | collective-permute-done | bytes 2097184 | tf_op jit(solution)/shard_map/ppermute | solution.py:50
  191.0 7.6 %add_convert_fusion = bf16[1024,1024]{1,0:T(8,128)(2,1)} fusion(bf16[1024,1024]{1,0:T(8,128)(2,1)} %collective-permute-done.2, bf16[1024,1024]{1,0:T(8,128)(2,1)} %param.12, bf16[1024,1024]{0,1:T(8,128)(2,1)} %bitcast.54, bf16[1024,2048]{1,0:T(8,128)(2,1)} %param.18, s32[]{:T(128)S(6)} %select_n.77), kind=kOutput, calls=%fused_computation.15 | convolution fusion | flops 2154823680 | bytes 10485764 | tf_op jit(solution)/shard_map/dot_general | solution.py:152
  (63 shorter events, 7.1 us)
Async XLA Ops:
  7.2 107.1 %copy-start = (bf16[512,2048]{1,0:T(8,128)(2,1)S(1)}, bf16[512,2048]{1,0:T(8,128)(2,1)}, u32[]{:S(2)}) copy-start(bf16[512,2048]{1,0:T(8,128)(2,1)} %param.17) | copy-start | bytes 6291460
  7.2 11.2 %copy-start.9 = (s32[1,4]{1,0:T(1,128)S(1)}, s32[1,4]{1,0:T(1,128)}, u32[]{:S(2)}) copy-start(s32[1,4]{1,0:T(1,128)} %param.22) | copy-start | bytes 52
  7.2 14.4 %copy-start.10 = (bf16[2048]{0:T(1024)(128)(2,1)S(1)}, bf16[2048]{0:T(1024)(128)(2,1)}, u32[]{:S(2)}) copy-start(bf16[2048]{0:T(1024)(128)(2,1)} %param.13) | copy-start | bytes 12292
  7.2 14.4 %copy-start.13 = (s32[1,4]{1,0:T(1,128)S(1)}, s32[1,4]{1,0:T(1,128)}, u32[]{:S(2)}) copy-start(s32[1,4]{1,0:T(1,128)} %param.21) | copy-start | bytes 52
  7.2 14.6 %copy-start.11 = (bf16[512]{0:T(512)(128)(2,1)S(1)}, bf16[512]{0:T(512)(128)(2,1)}, u32[]{:S(2)}) copy-start(bf16[512]{0:T(512)(128)(2,1)} %param.16) | copy-start | bytes 3076
  7.2 87.3 %all-gather.2.cloned.1.call-start = ((), (), s32[]{:S(2)}) async-start(), calls=%async_computation | async-start | bytes 9052160 | tf_op jit(solution)/shard_map/all_gather | solution.py:75
  9.0 16.3 %collective-permute-start = (bf16[1024,1024]{1,0:T(8,128)(2,1)}, bf16[1024,1024]{1,0:T(8,128)(2,1)}, u32[]{:S(2)}, u32[]{:S(2)}) collective-permute-start(bf16[1024,1024]{1,0:T(8,128)(2,1)} %param.12), channel_id=1, source_target_pairs={{0,1},{1,0},{2,3},{3,2},{4,5},{5,4},{6,7},{7,6},{8,9},{9,8},{10,11... | collective-permute-start | bytes 6291464 | tf_op jit(solution)/shard_map/ppermute | solution.py:50
  18.4 10.5 %collective-permute-start.1 = (bf16[2048,64]{1,0:T(8,128)(2,1)}, bf16[2048,64]{1,0:T(8,128)(2,1)}, u32[]{:S(2)}, u32[]{:S(2)}) collective-permute-start(bf16[2048,64]{1,0:T(8,128)(2,1)} %pad_maximum_fusion.2), channel_id=1, source_target_pairs={{0,1},{1,0},{2,3},{3,2},{4,5},{5,4},{6,7},{7,6},{8,9},{9,8},{10,11... | collective-permute-start | bytes 786440 | tf_op jit(solution)/shard_map/ppermute | solution.py:50
  27.8 4.2 %copy-start.3 = (bf16[1024,1024]{1,0:T(8,128)(2,1)}, bf16[1024,1024]{1,0:T(8,128)(2,1)S(1)}, u32[]{:S(2)}) copy-start(bf16[1024,1024]{1,0:T(8,128)(2,1)S(1)} %get-tuple-element.8) | copy-start | bytes 6291460
  27.8 4.2 %copy-start.4 = (bf16[1024,1024]{1,0:T(8,128)(2,1)}, bf16[1024,1024]{1,0:T(8,128)(2,1)S(1)}, u32[]{:S(2)}) copy-start(bf16[1024,1024]{1,0:T(8,128)(2,1)S(1)} %get-tuple-element.9) | copy-start | bytes 6291460
  114.3 2.4 %copy-start.5 = (bf16[1024,512]{0,1:T(8,128)(2,1)}, bf16[1024,512]{0,1:T(8,128)(2,1)S(1)}, u32[]{:S(2)}) copy-start(bf16[1024,512]{0,1:T(8,128)(2,1)S(1)} %multiply_convert_fusion) | copy-start | bytes 3145732
  116.7 3.2 %slice-start = ((s8[8650752]{0:T(1024)(128)(4,1)}), s8[262144]{0:T(1024)(128)(4,1)S(1)}, s32[]{:S(2)}) async-start(s8[8650752]{0:T(1024)(128)(4,1)} %bitcast.44), calls=%async_computation.1 | async-start | bytes 524288
  116.7 3.2 %slice-start.1 = ((s8[8650752]{0:T(1024)(128)(4,1)}), s8[4194304]{0:T(1024)(128)(4,1)S(1)}, s32[]{:S(2)}) async-start(s8[8650752]{0:T(1024)(128)(4,1)} %bitcast.44), calls=%async_computation.2 | async-start | bytes 8388608
  118.2 3.1 %slice-start.2 = ((s8[8650752]{0:T(1024)(128)(4,1)}), s8[4194304]{0:T(1024)(128)(4,1)S(1)}, s32[]{:S(2)}) async-start(s8[8650752]{0:T(1024)(128)(4,1)} %bitcast.44), calls=%async_computation.3 | async-start | bytes 8388608
  118.2 3.1 %copy-start.8 = (f32[1024]{0:T(1024)S(1)}, f32[1024]{0:T(1024)}, u32[]{:S(2)}) copy-start(f32[1024]{0:T(1024)} %subtract_convert_fusion.2) | copy-start | bytes 12292
  118.2 3.1 %copy-start.12 = (f32[32]{0:T(128)S(1)}, f32[32]{0:T(128)}, u32[]{:S(2)}) copy-start(f32[32]{0:T(128)} %multiply_exponential_fusion) | copy-start | bytes 388
  118.3 3.7 %copy-start.7 = (bf16[16,1536]{1,0:T(8,128)(2,1)S(1)}, bf16[16,1536]{1,0:T(8,128)(2,1)}, u32[]{:S(2)}) copy-start(bf16[16,1536]{1,0:T(8,128)(2,1)} %get-tuple-element.13) | copy-start | bytes 147460
  123.0 2.7 %copy-start.2 = (f32[1024,1536]{0,1:T(8,128)}, f32[1024,1536]{0,1:T(8,128)S(1)}, u32[]{:S(2)}) copy-start(f32[1024,1536]{0,1:T(8,128)S(1)} %slice_add_fusion) | copy-start | bytes 18874372
  180.1 6.7 %copy-start.6 = (bf16[1024,512]{0,1:T(8,128)(2,1)S(1)}, bf16[1024,512]{0,1:T(8,128)(2,1)}, u32[]{:S(2)}) copy-start(bf16[1024,512]{0,1:T(8,128)(2,1)} %copy-done.5) | copy-start | bytes 3145732
  186.1 4.8 %collective-permute-start.2 = (bf16[1024,1024]{1,0:T(8,128)(2,1)}, bf16[1024,1024]{1,0:T(8,128)(2,1)}, u32[]{:S(2)}, u32[]{:S(2)}) collective-permute-start(bf16[1024,1024]{1,0:T(8,128)(2,1)} %fusion.14), channel_id=1, source_target_pairs={{0,1},{1,0},{2,3},{3,2},{4,5},{5,4},{6,7},{7,6},{8,9},{9,8},{10,11... | collective-permute-start | bytes 6291464 | tf_op jit(solution)/shard_map/ppermute | solution.py:50
  191.0 7.6 %copy-start.1 = (bf16[512,2048]{1,0:T(8,128)(2,1)S(1)}, bf16[512,2048]{1,0:T(8,128)(2,1)}, u32[]{:S(2)}) copy-start(bf16[512,2048]{1,0:T(8,128)(2,1)} %param.17) | copy-start | bytes 6291460
Sparse Core Ops, SparseCore 0:
  10.8 83.6 all-gather.1
where the time goes:
time: 206 us; the launch traced here: 205 us
  matrix products  90.3 us (44%)
  waiting for transfers between devices  65.6 us (32%)
  between operations  19.2 us (9%)
  other arithmetic  15.3 us (7%)
  local copies, waits for them, and re-layouts  12.7 us (6%)
  starting transfers between devices  2.24 us (1%)
    all_gather x1, waiting for transfers between devices, body(): joined = lax.all_gather(joined, 'wide', axis=0, tiled=True)  62.5 us
    sub x1, matrix products, body(): expo = jnp.exp(scores - top)  26.8 us
    dot_general x1, matrix products, body(): projections = jnp.dot(normed, joined, preferred_element_type=jnp.float32)  16.1 us
    dot_general x1, matrix products, body(): jnp.einsum('hqk,khd->qhd', weights, values, preferred_element_type=jnp.fl...  14.1 us
    dot_general x1, matrix products, body(): jnp.einsum('qhd,kd->hqk', query_vectors[..., NOPE:], key_rope, preferred_...  13.2 us
    dot_general x1, matrix products, body(): jnp.dot(attended, my_cols, preferred_element_type=jnp.float32)  7.56 us
    dot_general x1, matrix products, body(): jnp.dot(attended, their_cols, preferred_element_type=jnp.float32)  6.02 us
    unnamed x35, local copies, waits for them, and re-layouts  5.77 us
  transfers between devices with their start and end apart: 4, of which 2 were waited for; matrix products, arithmetic and copies ran while one was open for 9% of the time, Pallas kernels for 0%

commit v1 on v0

--- a/solution.py
+++ b/solution.py
@@ -72,7 +72,10 @@
     me = lax.axis_index("narrow")
     mine_first = me == 0
     joined = jnp.concatenate([q_weight, kva_weight], axis=1)
-    joined = lax.all_gather(joined, "wide", axis=0, tiled=True)
+    peers = lax.axis_size("wide")
+    blocks = jnp.stack([joined for _ in range(peers)])
+    blocks = lax.all_to_all(blocks, "wide", split_axis=0, concat_axis=0)
+    joined = jnp.concatenate(blocks, axis=0)
     other = swap(tokens)
     whole = jnp.concatenate(
         [jnp.where(mine_first, tokens, other), jnp.where(mine_first, other, tokens)], axis=1

time: 206 us -> 255 us (1.24)
  the two profiles are of different devices: /device:TPU:1 before, /device:TPU:5 now
where the time goes in v1:
time: 255 us
  waiting for transfers between devices  114 us (45%)
  matrix products  90.3 us (35%)
  local copies, waits for them, and re-layouts  16.5 us (6%)
  starting transfers between devices  14.2 us (6%)
  other arithmetic  13.9 us (5%)
  between operations  5.87 us (2%)
    all_to_all x1, waiting for transfers between devices, body(): blocks = lax.all_to_all(blocks, 'wide', split_axis=0, concat_axis=0)  111 us
    sub x1, matrix products, body(): expo = jnp.exp(scores - top)  26.8 us
    dot_general x1, matrix products, body(): projections = jnp.dot(normed, joined, preferred_element_type=jnp.float32)  16.1 us
    dot_general x1, matrix products, body(): jnp.einsum('hqk,khd->qhd', weights, values, preferred_element_type=jnp.fl...  14.1 us
    dot_general x1, matrix products, body(): jnp.einsum('qhd,kd->hqk', query_vectors[..., NOPE:], key_rope, preferred_...  13.2 us
    all_to_all x1, starting transfers between devices, body(): blocks = lax.all_to_all(blocks, 'wide', split_axis=0, concat_axis=0)  11.2 us
    dot_general x1, matrix products, body(): jnp.dot(attended, my_cols, preferred_element_type=jnp.float32)  7.56 us
    dot_general x1, matrix products, body(): jnp.dot(attended, their_cols, preferred_element_type=jnp.float32)  6.02 us
  transfers between devices with their start and end apart: 4, of which 2 were waited for; matrix products, arithmetic and copies ran while one was open for 7% of the time, Pallas kernels for 0%

profile of v1, /device:TPU:5, one launch (start us, length us, event | category | flops | bytes accessed | tf_op | source)
XLA Modules:
  0.0 254.8 jit_solution(3985171504306650388)
XLA Ops:
  1.7 4.0 %stack.2 = bf16[64,32,2112]{2,1,0:T(8,128)(2,1)} broadcast(bf16[32,2112]{1,0:T(8,128)(2,1)S(1)} %pad_maximum_fusion.3), dimensions={1,2} | broadcast | bytes 8785920 | tf_op jit(solution)/shard_map/stack | solution.py:76
  5.8 11.2 %all-to-all-start = ((bf16[64,32,2112]{2,1,0:T(8,128)(2,1)}), bf16[64,32,2112]{2,1,0:T(8,128)(2,1)}, u32[]{:S(2)}, u32[]{:S(2)}) async-start(bf16[64,32,2112]{2,1,0:T(8,128)(2,1)} %stack.2), calls=%async_computation | async-start | bytes 17825792 | tf_op jit(solution)/shard_map/all_to_all | solution.py:77
  17.0 1.3 collective-permute-start
  21.7 2.2 constant_dynamic-slice_fusion.7
  23.9 1.5 pad_maximum_fusion.2
  30.1 1.5 constant_dynamic-slice_fusion.3
  32.2 2.5 broadcast_select_fusion.1
  35.8 3.1 %fusion.26 = f32[1024,64]{0,1:T(8,128)S(1)} fusion(bf16[2048,64]{1,0:T(8,128)(2,1)} %pad_maximum_fusion.2, bf16[2048,64]{1,0:T(8,128)(2,1)} %collective-permute-done.1, pred[64]{0:T(512)(128)(4,1)S(1)} %broadcast_in_dim.22, f32[2048]{0:T(1024)S(1)} %convert_element_type.94, f32[1024]{0:T(1024)S(1)} %add_rsqrt_fusion.1, ...), kind=kOutput, calls=%fused_computation.39 | convolution fusion | flops 283246592 | bytes 4993088 | tf_op jit(solution)/shard_map/dot_general | solution.py:108
  38.9 111.0 %all-to-all-done = bf16[64,32,2112]{2,1,0:T(8,128)(2,1)} async-done(((bf16[64,32,2112]{2,1,0:T(8,128)(2,1)}), bf16[64,32,2112]{2,1,0:T(8,128)(2,1)}, u32[]{:S(2)}, u32[]{:S(2)}) %all-to-all-start) | async-done | bytes 8650784 | tf_op jit(solution)/shard_map/all_to_all | solution.py:77
  149.9 16.1 %fusion.47 = f32[1024,2112]{0,1:T(8,128)} fusion(bf16[2048,2112]{1,0:T(8,128)(2,1)} %bitcast, f32[2048]{0:T(1024)S(1)} %convert_element_type.94, f32[1024]{0:T(1024)S(1)} %add_rsqrt_fusion.1, bf16[1024,1024]{1,0:T(8,128)(2,1)} %copy-done.4, bf16[1024,1024]{1,0:T(8,128)(2,1)} %copy-done.3), kind=kOutput, calls=%fused_computation.91 | convolution fusion | flops 8873050112 | bytes 21508096 | tf_op jit(solution)/shard_map/dot_general | solution.py:104
  166.0 1.8 multiply_reduce_fusion
  167.8 1.8 multiply_convert_fusion
  169.6 2.4 convolution_convert_fusion
  172.1 1.5 copy.40
  173.6 1.6 fusion.49
  175.2 1.5 slice-done.2
  178.4 2.7 %copy-done.2 = f32[1024,1536]{0,1:T(8,128)} copy-done((f32[1024,1536]{0,1:T(8,128)}, f32[1024,1536]{0,1:T(8,128)S(1)}, u32[]{:S(2)}) %copy-start.2) | copy-done | bytes 6291480
  181.4 13.2 %fusion.22 = f32[1024,1024,8]{1,0,2:T(8,128)} fusion(bf16[1024,8,32]{0,2,1:T(8,128)(2,1)S(1)} %get-tuple-element.5, bf16[1024,8,32]{0,2,1:T(8,128)(2,1)S(1)} %get-tuple-element.4, bf16[1024,32]{0,1:T(8,128)(2,1)S(1)} %get-tuple-element.3, bf16[1024,32]{0,1:T(8,128)(2,1)S(1)} %get-tuple-element.2), kind=kOutput, calls=%fused_computation.32 | convolution fusion | flops 1076101120 | bytes 34734080 | tf_op jit(solution)/shard_map/qhd,kd->hqk/dot_general | solution.py:138
  194.6 26.8 %fusion.52 = (f32[8,1024]{1,0:T(8,128)S(1)}, f32[8,1024,1024]{1,2,0:T(8,128)}) fusion(f32[1024,1024,8]{1,0,2:T(8,128)} %fusion.22, pred[1024,1024]{0,1:T(8,128)(4,1)S(1)} %fusion.7, f32[1024,8,192]{0,2,1:T(8,128)} %bitcast.44, bf16[1024,8,128]{2,1,0:T(8,128)(2,1)S(1)} %get-tuple-element.7), kind=kOutput, calls=%fused_computation.95 | convolution fusion | flops 2189427712 | bytes 72384512 | tf_op jit(solution)/shard_map/sub | solution.py:145
  221.3 14.1 %fusion.17 = bf16[8,128,1024]{2,1,0:T(8,128)(2,1)} fusion(f32[8,1024,1024]{1,2,0:T(8,128)} %get-tuple-element.31, f32[8,1024]{1,0:T(8,128)S(1)} %get-tuple-element.30, bf16[1024,8,128]{2,1,0:T(8,128)(2,1)} %get-tuple-element.6), kind=kOutput, calls=%fused_computation.30 | convolution fusion | flops 2165309440 | bytes 37781504 | tf_op jit(solution)/shard_map/hqk,khd->qhd/dot_general | solution.py:147
  235.5 6.0 %fusion.14 = bf16[1024,1024]{1,0:T(8,128)(2,1)} fusion(bf16[1024,1024]{0,1:T(8,128)(2,1)} %bitcast.54, bf16[1024,2048]{1,0:T(8,128)(2,1)} %param.18, s32[]{:T(128)S(6)} %select_n.78), kind=kOutput, calls=%fused_computation.29 | convolution fusion | flops 2148532224 | bytes 6291460 | tf_op jit(solution)/shard_map/dot_general | solution.py:153
  241.5 1.7 collective-permute-start.2
  244.2 3.0 %collective-permute-done.2 = bf16[1024,1024]{1,0:T(8,128)(2,1)} collective-permute-done((bf16[1024,1024]{1,0:T(8,128)(2,1)}, bf16[1024,1024]{1,0:T(8,128)(2,1)}, u32[]{:S(2)}, u32[]{:S(2)}) %collective-permute-start.2) | collective-permute-done | bytes 2097184 | tf_op jit(solution)/shard_map/ppermute | solution.py:50
  247.2 7.6 %add_convert_fusion = bf16[1024,1024]{1,0:T(8,128)(2,1)} fusion(bf16[1024,1024]{1,0:T(8,128)(2,1)} %collective-permute-done.2, bf16[1024,1024]{1,0:T(8,128)(2,1)} %param.12, bf16[1024,1024]{0,1:T(8,128)(2,1)} %bitcast.55, bf16[1024,2048]{1,0:T(8,128)(2,1)} %param.18, s32[]{:T(128)S(6)} %select_n.77), kind=kOutput, calls=%fused_computation.15 | convolution fusion | flops 2154823680 | bytes 10485764 | tf_op jit(solution)/shard_map/dot_general | solution.py:155
  (65 shorter events, 8.9 us)
Async XLA Ops:
  0.6 169.0 %copy-start = (bf16[512,2048]{1,0:T(8,128)(2,1)S(1)}, bf16[512,2048]{1,0:T(8,128)(2,1)}, u32[]{:S(2)}) copy-start(bf16[512,2048]{1,0:T(8,128)(2,1)} %param.17) | copy-start | bytes 6291460
  5.8 12.6 %copy-start.9 = (s32[1,4]{1,0:T(1,128)S(1)}, s32[1,4]{1,0:T(1,128)}, u32[]{:S(2)}) copy-start(s32[1,4]{1,0:T(1,128)} %param.22) | copy-start | bytes 52
  5.8 12.6 %copy-start.13 = (s32[64]{0:T(128)S(1)}, s32[64]{0:T(128)}, u32[]{:S(2)}) copy-start(s32[64]{0:T(128)} %param.23) | copy-start | bytes 772
  5.8 144.1 %all-to-all-start = ((bf16[64,32,2112]{2,1,0:T(8,128)(2,1)}), bf16[64,32,2112]{2,1,0:T(8,128)(2,1)}, u32[]{:S(2)}, u32[]{:S(2)}) async-start(bf16[64,32,2112]{2,1,0:T(8,128)(2,1)} %stack.2), calls=%async_computation | async-start | bytes 17825792 | tf_op jit(solution)/shard_map/all_to_all | solution.py:77
  17.0 11.6 %copy-start.10 = (bf16[2048]{0:T(1024)(128)(2,1)S(1)}, bf16[2048]{0:T(1024)(128)(2,1)}, u32[]{:S(2)}) copy-start(bf16[2048]{0:T(1024)(128)(2,1)} %param.13) | copy-start | bytes 12292
  17.0 11.6 %copy-start.14 = (s32[1,4]{1,0:T(1,128)S(1)}, s32[1,4]{1,0:T(1,128)}, u32[]{:S(2)}) copy-start(s32[1,4]{1,0:T(1,128)} %param.21) | copy-start | bytes 52
  17.0 11.8 %copy-start.11 = (bf16[512]{0:T(512)(128)(2,1)S(1)}, bf16[512]{0:T(512)(128)(2,1)}, u32[]{:S(2)}) copy-start(bf16[512]{0:T(512)(128)(2,1)} %param.16) | copy-start | bytes 3076
  17.0 15.2 %collective-permute-start = (bf16[1024,1024]{1,0:T(8,128)(2,1)}, bf16[1024,1024]{1,0:T(8,128)(2,1)}, u32[]{:S(2)}, u32[]{:S(2)}) collective-permute-start(bf16[1024,1024]{1,0:T(8,128)(2,1)} %param.12), channel_id=1, source_target_pairs={{0,1},{1,0},{2,3},{3,2},{4,5},{5,4},{6,7},{7,6},{8,9},{9,8},{10,11... | collective-permute-start | bytes 6291464 | tf_op jit(solution)/shard_map/ppermute | solution.py:50
  25.4 10.4 %collective-permute-start.1 = (bf16[2048,64]{1,0:T(8,128)(2,1)}, bf16[2048,64]{1,0:T(8,128)(2,1)}, u32[]{:S(2)}, u32[]{:S(2)}) collective-permute-start(bf16[2048,64]{1,0:T(8,128)(2,1)} %pad_maximum_fusion.2), channel_id=1, source_target_pairs={{0,1},{1,0},{2,3},{3,2},{4,5},{5,4},{6,7},{7,6},{8,9},{9,8},{10,11... | collective-permute-start | bytes 786440 | tf_op jit(solution)/shard_map/ppermute | solution.py:50
  34.7 4.1 %copy-start.3 = (bf16[1024,1024]{1,0:T(8,128)(2,1)}, bf16[1024,1024]{1,0:T(8,128)(2,1)S(1)}, u32[]{:S(2)}) copy-start(bf16[1024,1024]{1,0:T(8,128)(2,1)S(1)} %get-tuple-element.8) | copy-start | bytes 6291460
  34.7 4.1 %copy-start.4 = (bf16[1024,1024]{1,0:T(8,128)(2,1)}, bf16[1024,1024]{1,0:T(8,128)(2,1)S(1)}, u32[]{:S(2)}) copy-start(bf16[1024,1024]{1,0:T(8,128)(2,1)S(1)} %get-tuple-element.9) | copy-start | bytes 6291460
  169.6 2.4 copy-start.5
  172.0 3.2 %slice-start = ((s8[8650752]{0:T(1024)(128)(4,1)}), s8[262144]{0:T(1024)(128)(4,1)S(1)}, s32[]{:S(2)}) async-start(s8[8650752]{0:T(1024)(128)(4,1)} %bitcast.45), calls=%async_computation.1 | async-start | bytes 524288
  172.1 3.2 %slice-start.1 = ((s8[8650752]{0:T(1024)(128)(4,1)}), s8[4194304]{0:T(1024)(128)(4,1)S(1)}, s32[]{:S(2)}) async-start(s8[8650752]{0:T(1024)(128)(4,1)} %bitcast.45), calls=%async_computation.2 | async-start | bytes 8388608
  173.6 3.1 %slice-start.2 = ((s8[8650752]{0:T(1024)(128)(4,1)}), s8[4194304]{0:T(1024)(128)(4,1)S(1)}, s32[]{:S(2)}) async-start(s8[8650752]{0:T(1024)(128)(4,1)} %bitcast.45), calls=%async_computation.3 | async-start | bytes 8388608
  173.6 3.1 %copy-start.8 = (f32[1024]{0:T(1024)S(1)}, f32[1024]{0:T(1024)}, u32[]{:S(2)}) copy-start(f32[1024]{0:T(1024)} %subtract_convert_fusion.2) | copy-start | bytes 12292
  173.6 3.1 %copy-start.12 = (f32[32]{0:T(128)S(1)}, f32[32]{0:T(128)}, u32[]{:S(2)}) copy-start(f32[32]{0:T(128)} %multiply_exponential_fusion) | copy-start | bytes 388
  173.6 3.7 %copy-start.7 = (bf16[16,1536]{1,0:T(8,128)(2,1)S(1)}, bf16[16,1536]{1,0:T(8,128)(2,1)}, u32[]{:S(2)}) copy-start(bf16[16,1536]{1,0:T(8,128)(2,1)} %get-tuple-element.13) | copy-start | bytes 147460
  178.4 2.7 %copy-start.2 = (f32[1024,1536]{0,1:T(8,128)}, f32[1024,1536]{0,1:T(8,128)S(1)}, u32[]{:S(2)}) copy-start(f32[1024,1536]{0,1:T(8,128)S(1)} %slice_add_fusion) | copy-start | bytes 18874372
  235.4 7.7 %copy-start.6 = (bf16[1024,512]{0,1:T(8,128)(2,1)S(1)}, bf16[1024,512]{0,1:T(8,128)(2,1)}, u32[]{:S(2)}) copy-start(bf16[1024,512]{0,1:T(8,128)(2,1)} %copy-done.5) | copy-start | bytes 3145732
  241.5 5.8 %collective-permute-start.2 = (bf16[1024,1024]{1,0:T(8,128)(2,1)}, bf16[1024,1024]{1,0:T(8,128)(2,1)}, u32[]{:S(2)}, u32[]{:S(2)}) collective-permute-start(bf16[1024,1024]{1,0:T(8,128)(2,1)} %fusion.14), channel_id=1, source_target_pairs={{0,1},{1,0},{2,3},{3,2},{4,5},{5,4},{6,7},{7,6},{8,9},{9,8},{10,11... | collective-permute-start | bytes 6291464 | tf_op jit(solution)/shard_map/ppermute | solution.py:50
  247.2 7.6 %copy-start.1 = (bf16[512,2048]{1,0:T(8,128)(2,1)S(1)}, bf16[512,2048]{1,0:T(8,128)(2,1)}, u32[]{:S(2)}) copy-start(bf16[512,2048]{1,0:T(8,128)(2,1)} %param.17) | copy-start | bytes 6291460
